TPU v7x, 512 devices: a whole 4x8x8 slice. The times are simulated.
512 devices in a mesh: atom: 64 (over y, x, z_hi), ka: 8 (over z_lo, core).
Axes of the slice: x: 4, y: 8, z: 8 (z_hi: 2, z_lo: 4; z = z_hi * 4 + z_lo), core: 2. Of those that a mesh axis runs over, the one named last changes fastest.
Arguments:
- features: bfloat16 [131072, 256], P('atom'), may hold values from -6 to 6
- positions: float32 [3, 131072], P(None, 'atom'), may hold values from 0 to 1
- k_indices: int32 [3, 4096], P(None, 'ka'), may hold values from -8 to 8
- species: int32 [131072], P('atom'), may hold values from 0 to 7
- brick_counts: int32 [64], P('atom'), may hold values from 1024 to 2048, as said below
- smearing: float32 [256], replicated, may hold values from 0.01 to 0.03
- teacher_charge: float32 [256], replicated, may hold values from -0.375 to 0.375
- norm_gain: float32 [256], replicated, may hold values from 0.5 to 1.5
- w_mix: bfloat16 [256, 256], replicated, may hold values from -0.375 to 0.375
- w_read: float32 [256], replicated, may hold values from -0.375 to 0.375
- w_student: bfloat16 [256, 128], replicated, may hold values from -0.375 to 0.375
- species_embed: float32 [8, 128], replicated, may hold values from -3 to 3
- w_charge: float32 [128], replicated, may hold values from -0.5 to 0.5
- species_bias: float32 [8], replicated, may hold values from -3 to 3
- student_smear: float32 [1], replicated, may hold values from 0.05 to 0.15
Outputs:
- teacher_features: bfloat16 [131072, 256], P(('atom', 'ka'))
- teacher_forces: float32 [3, 131072], P(None, ('atom', 'ka'))
- student_forces: float32 [3, 131072], P(None, ('atom', 'ka'))
- student_energy: float32 [131072], P(('atom', 'ka'))
- distill_loss: float32 [], replicated
Inputs may be any that keep to these rules, and one draw needn't show every extreme that they name: The first brick_counts[b] atom slots of brick b hold real atoms and the rest are padding; some brick is full in every draw.
All inputs are finite; a program needn't handle non-finite values.
Results may differ from a plain program's by a relative error of at most 0.0075.
Values sent between devices are 32-bit elements; how exact they have to be, the bound alone decides.
No kernel may reach another device: no remote copies, remote signals or barrier semaphores. Data moves between devices by JAX's collectives and lax.ppermute only.
A program may use at most 64 MiB of HBM per device.

v0:
```python
import functools
import math
import jax
import jax.numpy as jnp
from jax import lax
from jax.sharding import Mesh
from jax.sharding import PartitionSpec as P

TWO_PI = 2.0 * math.pi
SCREEN = 20.0
HIGHEST_PRECISION = lax.Precision.HIGHEST
ATOM_AXES = ("y", "x", "zh")
KA_AXES = ("zl", "core")
ALL_AXES = ATOM_AXES + KA_AXES
PAD_ROWS = 256


def phase_table(positions, k_indices):
    k_float = k_indices.astype(jnp.float32)
    products = (
        positions[0][:, None] * k_float[0][None, :]
        + positions[1][:, None] * k_float[1][None, :]
        + positions[2][:, None] * k_float[2][None, :]
    )
    angles = TWO_PI * products
    return jnp.concatenate([jnp.cos(angles), jnp.sin(angles)], axis=1).astype(jnp.bfloat16)


def k_geometry(k_indices):
    k_vectors = TWO_PI * k_indices.astype(jnp.float32)
    k_square = (
        k_vectors[0] * k_vectors[0] + k_vectors[1] * k_vectors[1] + k_vectors[2] * k_vectors[2]
    )
    return (k_vectors, k_square)


def teacher_kernel(k_square, smearing, inv_root):
    spread = (smearing * smearing)[None, :]
    return jnp.exp(-0.5 * k_square[:, None] * spread) / (k_square[:, None] + SCREEN) * inv_root


def student_table(k_vectors, k_square, sums, student_smear, inv_root, k_width):
    spread = student_smear[0] * student_smear[0]
    kernel = jnp.exp(-0.5 * k_square * spread) / (k_square + SCREEN) * inv_root
    cos_part = kernel * sums[:k_width]
    sin_part = kernel * sums[k_width:]
    upper_rows = jnp.stack(
        [
            cos_part,
            -(k_vectors[0] * sin_part),
            -(k_vectors[1] * sin_part),
            -(k_vectors[2] * sin_part),
        ],
        axis=1,
    )
    lower_rows = jnp.stack(
        [sin_part, k_vectors[0] * cos_part, k_vectors[1] * cos_part, k_vectors[2] * cos_part],
        axis=1,
    )
    return jnp.concatenate([upper_rows, lower_rows], axis=0).astype(jnp.bfloat16)


def student_charge(features, species, live_mask, w_student, species_embed, w_charge, species_bias):
    onehot = (
        species[:, None] == jnp.arange(species_embed.shape[0], dtype=jnp.int32)[None, :]
    ).astype(jnp.float32)
    inner_sum = jnp.dot(features, w_student, preferred_element_type=jnp.float32) + jnp.dot(
        onehot, species_embed, precision=HIGHEST_PRECISION
    )
    hidden = jax.nn.silu(inner_sum)
    return (
        jnp.dot(hidden, w_charge, precision=HIGHEST_PRECISION)
        + jnp.dot(onehot, species_bias, precision=HIGHEST_PRECISION)
    ) * live_mask


def finish(
    potential, teacher_force, student_part, features, charge, live_mask, norm_gain, w_mix, w_read
):
    mean_square = jnp.mean(potential * potential, axis=1, keepdims=True)
    normed = (potential * lax.rsqrt(mean_square + 1e-06) * norm_gain[None, :]).astype(jnp.bfloat16)
    update = jax.nn.silu(jnp.dot(normed, w_mix, preferred_element_type=jnp.float32))
    combined = features.astype(jnp.float32) + update
    teacher_energy = jnp.dot(combined, w_read, precision=HIGHEST_PRECISION)
    student_energy = 0.5 * charge * student_part[:, 0]
    forces = charge[:, None] * student_part[:, 1:4]
    misfit = (student_energy - teacher_energy) ** 2 + jnp.sum(
        (forces - teacher_force) ** 2, axis=1
    ) / 3.0
    return (
        combined.astype(jnp.bfloat16),
        teacher_force,
        forces,
        student_energy,
        live_mask * misfit,
    )


def sum_over_atoms(payload):
    part = lax.psum_scatter(payload, "y", scatter_dimension=0, tiled=True)
    part = lax.psum_scatter(part, "x", scatter_dimension=0, tiled=True)
    part = lax.psum(part, "zh")
    part = lax.all_gather(part, "x", axis=0, tiled=True)
    return lax.all_gather(part, "y", axis=0, tiled=True)


def local(
    features,
    positions,
    k_indices,
    species,
    brick_counts,
    smearing,
    teacher_charge,
    norm_gain,
    w_mix,
    w_read,
    w_student,
    species_embed,
    w_charge,
    species_bias,
    student_smear,
):
    atom_rows = features.shape[0]
    k_width = k_indices.shape[1]
    channels = features.shape[1]
    atom_groups = 1
    for axis in ATOM_AXES:
        atom_groups *= lax.axis_size(axis)
    ka_groups = 1
    for axis in KA_AXES:
        ka_groups *= lax.axis_size(axis)
    inv_root = 1.0 / math.sqrt(atom_rows * atom_groups)
    live_mask = (jnp.arange(atom_rows, dtype=jnp.int32) < brick_counts[0]).astype(jnp.float32)
    masked = features * live_mask.astype(jnp.bfloat16)[:, None]
    charge = student_charge(
        features, species, live_mask, w_student, species_embed, w_charge, species_bias
    )
    charge_low = charge.astype(jnp.bfloat16)
    phases = phase_table(positions, k_indices)
    factor = lax.dot_general(
        phases, masked, (((0,), (0,)), ((), ())), preferred_element_type=jnp.float32
    )
    charge_sum = jnp.dot(charge_low, phases, preferred_element_type=jnp.float32)
    extra = jnp.concatenate(
        [
            charge_sum,
            brick_counts.astype(jnp.float32),
            jnp.zeros((PAD_ROWS * channels - 2 * k_width - 1,), jnp.float32),
        ]
    ).reshape(PAD_ROWS, channels)
    summed = sum_over_atoms(jnp.concatenate([factor, extra], axis=0))
    factor = summed[: 2 * k_width]
    extra = summed[2 * k_width :].reshape(-1)
    charge_sum = extra[: 2 * k_width]
    live_total = extra[2 * k_width]
    k_vectors, k_square = k_geometry(k_indices)
    kernel = teacher_kernel(k_square, smearing, inv_root)
    weighted = (jnp.concatenate([kernel, kernel], axis=0) * factor).astype(jnp.bfloat16)
    potential = jnp.dot(phases, weighted, preferred_element_type=jnp.float32)
    charged = (features.astype(jnp.float32) * teacher_charge[None, :]).astype(jnp.bfloat16)
    contracted = lax.dot_general(
        charged, weighted, (((1,), (1,)), ((), ())), preferred_element_type=jnp.float32
    )
    cosines = phases[:, :k_width].astype(jnp.float32)
    sines = phases[:, k_width:].astype(jnp.float32)
    force_terms = sines * contracted[:, :k_width] - cosines * contracted[:, k_width:]
    teacher_force = jnp.dot(force_terms, k_vectors.T, precision=HIGHEST_PRECISION)
    table = student_table(k_vectors, k_square, charge_sum, student_smear, inv_root, k_width)
    student_part = jnp.dot(phases, table, preferred_element_type=jnp.float32)
    packed = jnp.concatenate(
        [potential, teacher_force, student_part, jnp.zeros((atom_rows, 1), jnp.float32)], axis=1
    )
    own = lax.psum_scatter(packed, KA_AXES, scatter_dimension=0, tiled=True)
    share_rows = atom_rows // ka_groups
    ka_index = lax.axis_index(KA_AXES)
    row_start = ka_index * share_rows

    def own_rows(values):
        return lax.dynamic_slice_in_dim(values, row_start, share_rows, 0)

    teacher_features, teacher_out, forces, student_energy, misfit = finish(
        own[:, :channels],
        own[:, channels : channels + 3],
        own[:, channels + 3 : channels + 7],
        own_rows(features),
        own_rows(charge),
        own_rows(live_mask),
        norm_gain,
        w_mix,
        w_read,
    )
    loss_sum = functools.reduce(lambda v, axis: lax.psum(v, axis), ALL_AXES, jnp.sum(misfit))
    return (teacher_features, teacher_out.T, forces.T, student_energy, loss_sum / live_total)


def solution(mesh):
    sizes = dict(mesh.shape)
    ka = sizes["ka"]
    atom = sizes["atom"]
    cores = 2
    z_lo = ka // cores
    devices = mesh.devices.reshape(-1)
    y_size = 8 if atom % 8 == 0 else 1
    rest = atom // y_size
    zh = 2 if rest % 2 == 0 else 1
    x_size = rest // zh
    fine = Mesh(devices.reshape(y_size, x_size, zh, z_lo, cores), ALL_AXES)
    atom_spec = ATOM_AXES
    in_specs = (
        P(atom_spec, None),
        P(None, atom_spec),
        P(None, KA_AXES),
        P(atom_spec),
        P(atom_spec),
        P(),
        P(),
        P(),
        P(),
        P(),
        P(),
        P(),
        P(),
        P(),
        P(),
    )
    out_specs = (P(ALL_AXES, None), P(None, ALL_AXES), P(None, ALL_AXES), P(ALL_AXES), P())
    return jax.shard_map(local, mesh=fine, in_specs=in_specs, out_specs=out_specs, check_vma=False)
```

profile of v0, /device:TPU:1, one launch (start us, length us, event | category | flops | bytes accessed | tf_op | source)
XLA Modules:
  0.0 326.0 jit_solution(14616286438022679318)
XLA Ops:
  7.2 0.9 fusion.66
  8.1 0.7 convert_element_type.52
  9.5 1.6 fusion.69
  11.2 1.4 fusion.14
  12.6 1.7 convolution_add_fusion
  14.3 1.2 fusion.8
  15.5 0.6 fusion.65
  16.2 17.6 %cosine_convert_fusion = (bf16[2048,512]{1,0:T(8,128)(2,1)S(1)}, bf16[2048,512]{1,0:T(8,128)(2,1)S(1)}) fusion(f32[512]{0:T(512)S(1)} %bitcast.109, f32[2048]{0:T(1024)S(1)} %bitcast.101, f32[512]{0:T(512)S(1)} %bitcast.111, f32[2048]{0:T(1024)S(1)} %bitcast.103, f32[512]{0:T(512)S(1)} %bitcast.107, f32[2048]{0:T(1024)S(1)} %bitcast.99), kind=kLoop, calls=%fused_computation.8 | loop fusion | flops 8388608 | bytes 4225024 | tf_op jit(solution)/shard_map/slice | solution.py:165
  33.8 1.3 copy-done.4
  35.2 0.6 fusion.60
  35.8 3.0 concatenate.22
  38.9 1.0 reshape.316
  39.9 3.2 fusion.15
  43.2 1.1 pad_maximum_fusion.1
  44.3 0.0 reduce-scatter.6.cloned.1.call-start
  44.4 43.4 %reduce-scatter.4.cloned.1.call-done = f32[160,256]{1,0:T(8,128)} async-done(((f32[1280,256]{1,0:T(8,128)}), f32[160,256]{1,0:T(8,128)}) %reduce-scatter.4.cloned.1.call-update) | async-done | bytes 163856 | tf_op jit(solution)/shard_map/reduce_scatter | solution.py:100
  87.8 0.0 all-gather.2.cloned.1.call-start
  87.8 29.4 %reduce-scatter.6.cloned.1.call-done = f32[40,256]{1,0:T(8,128)} async-done(((f32[160,256]{1,0:T(8,128)}), f32[40,256]{1,0:T(8,128)}) %reduce-scatter.6.cloned.1.call-update) | async-done | bytes 40976 | tf_op jit(solution)/shard_map/reduce_scatter | solution.py:101
  117.2 16.1 %psum.42 = f32[40,256]{1,0:T(8,128)S(1)} all-reduce(f32[40,256]{1,0:T(8,128)} %reduce-scatter.6.cloned.1.call-done), channel_id=1, replica_groups=mesh['y'=8,'x'=4,'zh'=2,'zl'=4,'core'=2] {'zh'}, use_global_device_ids=true, to_apply=%region_2.3 | all-reduce | flops 10240 | bytes 81920 | tf_op jit(solution)/shard_map/psum | solution.py:102
  133.3 9.9 %all_gather.6 = f32[160,256]{1,0:T(8,128)} all-gather(f32[40,256]{1,0:T(8,128)S(1)} %psum.42), channel_id=1, replica_groups=mesh['y'=8,'x'=4,'zh'=2,'zl'=4,'core'=2] {'x'}, dimensions={0}, use_global_device_ids=true | all-gather | bytes 204800 | tf_op jit(solution)/shard_map/all_gather | solution.py:103
  143.2 0.2 reduce-scatter.8.cloned.1.call-start
  144.1 0.8 mul.545
  144.9 0.1 pad.3.clone
  144.9 0.7 broadcast_multiply_fusion
  145.7 0.2 divide_multiply_fusion
  145.9 36.9 %all-gather.2.cloned.1.call-done = f32[1280,256]{1,0:T(8,128)} async-done(((f32[160,256]{1,0:T(8,128)}), f32[1280,256]{1,0:T(8,128)}) %all-gather.2.cloned.1.call-update) | async-done | bytes 1310736 | tf_op jit(solution)/shard_map/all_gather | solution.py:104
  182.8 0.8 slice_bitcast_fusion.2
  183.7 2.5 fusion.5
  186.3 20.6 %fusion.1 = f32[2048,3]{0,1:T(4,128)S(1)} fusion(f32[2048,1024]{1,0:T(8,128)S(1)} %fusion.5, s32[3,512]{1,0:T(4,128)S(1)} %copy-done.9, f32[512]{0:T(512)S(1)} %bitcast.110, f32[2048]{0:T(1024)S(1)} %bitcast.102, f32[512]{0:T(512)S(1)} %bitcast.112, f32[2048]{0:T(1024)S(1)} %bitcast.104, f32[512]{0:T(512)S(1)} %bitcast.108, f32[2048]{0:T(1024)S(1)} %bitcast.100), kind=kOutput, calls=%fused_computation.2 | convolution fusion | flops 51383296 | bytes 8450048 | tf_op jit(solution)/shard_map/dot_general | solution.py:168
  207.0 1.2 fusion.24
  208.2 0.1 copy-done.6
  208.3 1.3 fusion.59
  209.7 1.6 maximum_maximum_fusion
  211.3 0.8 dynamic_slice.10
  212.0 44.2 %reduce-scatter.8.cloned.1.call-done = f32[256,264]{0,1:T(8,128)} async-done(((f32[2048,264]{0,1:T(8,128)}), f32[256,264]{0,1:T(8,128)}) %reduce-scatter.8.cloned.1.call-update) | async-done | bytes 270352 | tf_op jit(solution)/shard_map/reduce_scatter | solution.py:174
  256.2 1.0 multiply_reduce_fusion
  257.2 2.0 fusion.68
  259.2 0.3 fusion.70
  259.5 0.8 slice.127
  260.2 1.4 multiply_reduce_fusion.1
  261.6 1.9 multiply_reduce_fusion.2
  263.5 13.9 %psum.43 = f32[]{:T(128)} all-reduce(f32[]{:T(128)} %get-tuple-element.5), channel_id=1, replica_groups=mesh['y'=8,'x'=4,'zh'=2,'zl'=4,'core'=2] {'y'}, use_global_device_ids=true, to_apply=%region_7.8 | all-reduce | flops 1 | bytes 8 | tf_op jit(solution)/shard_map/psum | solution.py:193
  277.4 9.0 %psum.44 = f32[]{:T(128)} all-reduce(f32[]{:T(128)} %psum.43), channel_id=1, replica_groups=mesh['y'=8,'x'=4,'zh'=2,'zl'=4,'core'=2] {'x'}, use_global_device_ids=true, to_apply=%region_8.9 | all-reduce | flops 1 | bytes 8 | tf_op jit(solution)/shard_map/psum | solution.py:193
  286.5 8.3 %psum.45 = f32[]{:T(128)} all-reduce(f32[]{:T(128)} %psum.44), channel_id=1, replica_groups=mesh['y'=8,'x'=4,'zh'=2,'zl'=4,'core'=2] {'zh'}, use_global_device_ids=true, to_apply=%region_9.10 | all-reduce | flops 1 | bytes 8 | tf_op jit(solution)/shard_map/psum | solution.py:193
  294.8 0.1 copy.22
  294.9 11.2 %psum.46 = f32[]{:T(128)} all-reduce(f32[]{:T(128)} %psum.45), channel_id=1, replica_groups=mesh['y'=8,'x'=4,'zh'=2,'zl'=4,'core'=2] {'zl'}, use_global_device_ids=true, to_apply=%region_10.11 | all-reduce | flops 1 | bytes 8 | tf_op jit(solution)/shard_map/psum | solution.py:193
  306.2 0.5 slice.129
  306.7 10.5 %psum.47 = f32[]{:T(128)} all-reduce(f32[]{:T(128)} %psum.46), channel_id=1, replica_groups=mesh['y'=8,'x'=4,'zh'=2,'zl'=4,'core'=2] {'core'}, use_global_device_ids=true, to_apply=%region_11.12 | all-reduce | flops 1 | bytes 8 | tf_op jit(solution)/shard_map/psum | solution.py:193
  (55 shorter events, 0.4 us)
Async XLA Ops:
  7.2 250.0 %copy-start = (bf16[256,256]{1,0:T(8,128)(2,1)S(1)}, bf16[256,256]{1,0:T(8,128)(2,1)}, u32[]{:S(2)}) copy-start(bf16[256,256]{1,0:T(8,128)(2,1)} %param.23) | copy-start | bytes 393220
  7.2 7.1 %copy-start.18 = (f32[128]{0:T(128)S(1)}, f32[128]{0:T(128)}, u32[]{:S(2)}) copy-start(f32[128]{0:T(128)} %param.27) | copy-start | bytes 1540
  7.2 80.6 %reduce-scatter.4.cloned.1.call-start = ((), (), s32[]{:S(2)}) async-start(), calls=%async_computation.3 | async-start | bytes 1474560 | tf_op jit(solution)/shard_map/reduce_scatter | solution.py:100
  8.1 8.0 %copy-start.7 = (f32[1,2048]{1,0:T(1,128)}, f32[1,2048]{1,0:T(1,128)S(1)}, u32[]{:S(2)}) copy-start(f32[1,2048]{1,0:T(1,128)S(1)} %get-tuple-element.23) | copy-start | bytes 24580
  8.9 7.3 %copy-start.10 = (f32[1,512]{1,0:T(1,128)}, f32[1,512]{1,0:T(1,128)S(1)}, u32[]{:S(2)}) copy-start(f32[1,512]{1,0:T(1,128)S(1)} %get-tuple-element.34) | copy-start | bytes 6148
  8.9 7.3 %copy-start.12 = (f32[1,512]{1,0:T(1,128)}, f32[1,512]{1,0:T(1,128)S(1)}, u32[]{:S(2)}) copy-start(f32[1,512]{1,0:T(1,128)S(1)} %get-tuple-element.35) | copy-start | bytes 6148
  8.9 7.3 %copy-start.14 = (f32[1,512]{1,0:T(1,128)}, f32[1,512]{1,0:T(1,128)S(1)}, u32[]{:S(2)}) copy-start(f32[1,512]{1,0:T(1,128)S(1)} %get-tuple-element.36) | copy-start | bytes 6148
  33.8 1.3 copy-start.4
  33.8 9.3 %copy-start.2 = (bf16[2048,512]{1,0:T(8,128)(2,1)}, bf16[2048,512]{1,0:T(8,128)(2,1)S(1)}, u32[]{:S(2)}) copy-start(bf16[2048,512]{1,0:T(8,128)(2,1)S(1)} %get-tuple-element.24) | copy-start | bytes 6291460
  33.8 6.1 %copy-start.1 = (bf16[2048,256]{1,0:T(8,128)(2,1)S(1)}, bf16[2048,256]{1,0:T(8,128)(2,1)}, u32[]{:S(2)}) copy-start(bf16[2048,256]{1,0:T(8,128)(2,1)} %param.15) | copy-start | bytes 3145732
  44.3 72.9 %reduce-scatter.6.cloned.1.call-start = ((), (), s32[]{:S(2)}) async-start(), calls=%async_computation.4 | async-start | bytes 204800 | tf_op jit(solution)/shard_map/reduce_scatter | solution.py:101
  87.8 95.0 %all-gather.2.cloned.1.call-start = ((), (), s32[]{:S(2)}) async-start(), calls=%async_computation.5 | async-start | bytes 1474560 | tf_op jit(solution)/shard_map/all_gather | solution.py:104
  143.2 113.0 %reduce-scatter.8.cloned.1.call-start = ((), (), s32[]{:S(2)}) async-start(), calls=%async_computation.6 | async-start | bytes 2433024 | tf_op jit(solution)/shard_map/reduce_scatter | solution.py:174
  183.6 2.6 copy-start.8
  183.6 2.6 copy-start.9
  183.6 2.6 copy-start.11
  183.6 2.6 copy-start.13
  183.6 2.6 copy-start.15
  186.3 20.7 %copy-start.3 = (bf16[2048,512]{1,0:T(8,128)(2,1)S(1)}, bf16[2048,512]{1,0:T(8,128)(2,1)}, u32[]{:S(2)}) copy-start(bf16[2048,512]{1,0:T(8,128)(2,1)} %copy-done.2) | copy-start | bytes 6291460
  186.3 20.7 %copy-start.5 = (bf16[2048,512]{1,0:T(8,128)(2,1)S(1)}, bf16[2048,512]{1,0:T(8,128)(2,1)}, u32[]{:S(2)}) copy-start(bf16[2048,512]{1,0:T(8,128)(2,1)} %copy-done.4) | copy-start | bytes 6291460
  207.0 1.3 copy-start.6
  209.6 47.6 %copy-start.17 = (f32[256]{0:T(256)S(1)}, f32[256]{0:T(256)}, u32[]{:S(2)}) copy-start(f32[256]{0:T(256)} %param.22) | copy-start | bytes 3076
  209.7 49.5 %copy-start.16 = (f32[256]{0:T(256)S(1)}, f32[256]{0:T(256)}, u32[]{:S(2)}) copy-start(f32[256]{0:T(256)} %param.24) | copy-start | bytes 3076
Sparse Core Ops, SparseCore 0:
  44.5 43.2 reduce-scatter.3
  90.6 26.6 reduce-scatter.5
  143.3 39.4 all-gather.1
  211.4 44.7 reduce-scatter.7
where the time goes:
time: 327 us; the launch traced here: 326 us
  waiting for transfers between devices  154 us (47%)
  blocking collectives  79 us (24%)
  matrix products  37.7 us (12%)
  other arithmetic  27.7 us (8%)
  between operations  17.9 us (5%)
  local copies, waits for them, and re-layouts  9.57 us (3%)
    psum x5, blocking collectives, local(): lax.psum(v, axis)  53 us
    reduce_scatter x1, waiting for transfers between devices, local(): own = lax.psum_scatter(packed, KA_AXES, scatter_dimension=0, tiled=True)  44.2 us
    reduce_scatter x1, waiting for transfers between devices, sum_over_atoms(): part = lax.psum_scatter(payload, 'y', scatter_dimension=0, tiled=True)  43.4 us
    all_gather x1, waiting for transfers between devices, sum_over_atoms(): return lax.all_gather(part, 'y', axis=0, tiled=True)  36.9 us
    reduce_scatter x1, waiting for transfers between devices, sum_over_atoms(): part = lax.psum_scatter(part, 'x', scatter_dimension=0, tiled=True)  29.4 us
    dot_general x1, matrix products, local(): jnp.dot(force_terms, k_vectors.T, precision=HIGHEST_PRECISION)  20.6 us
    slice x1, other arithmetic, local(): cosines = phases[:, :k_width].astype(jnp.float32)  17.6 us
    psum x1, blocking collectives, sum_over_atoms(): part = lax.psum(part, 'zh')  16.1 us
  transfers between devices with their start and end apart: 4, of which 4 were waited for; matrix products, arithmetic and copies ran while one was open for 1% of the time, Pallas kernels for 0%

commit v1 on v0

--- a/solution.py
+++ b/solution.py
@@ -101,7 +101,10 @@
     part = lax.psum_scatter(part, "x", scatter_dimension=0, tiled=True)
     part = lax.psum(part, "zh")
     part = lax.all_gather(part, "x", axis=0, tiled=True)
-    return lax.all_gather(part, "y", axis=0, tiled=True)
+    prepare_stocks = lambda local_x, which_axis: jnp.concatenate(
+        lax.all_to_all(jnp.stack([local_x] * lax.axis_size(which_axis)), which_axis, 0, 0), axis=0
+    )
+    return prepare_stocks(part, "y")
 
 
 def local(

time: 327 us -> 316 us (0.966)
  waiting for transfers between devices: 154 us -> 137 us
  starting transfers between devices: 0.34 us -> 6.59 us
    all_gather x1 -> x0, waiting for transfers between devices: 36.9 us -> none  [sum_over_atoms(): return lax.all_gather(part, 'y', axis=0, tiled=True)]
    all_to_all x0 -> x1, waiting for transfers between devices: none -> 28.8 us  [sum_over_atoms(): lax.all_to_all(jnp.stack([local_x] * lax.axis_size(which_axis)), which_ax...]
    reduce_scatter x1, waiting for transfers between devices: 44.2 us -> 35.5 us  [local(): own = lax.psum_scatter(packed, KA_AXES, scatter_dimension=0, tiled=True)]
    all_to_all x0 -> x1, starting transfers between devices: none -> 6.48 us  [sum_over_atoms(): lax.all_to_all(jnp.stack([local_x] * lax.axis_size(which_axis)), which_ax...]
  transfers between devices with their start and end apart: 4 -> 4, of which waited for: 4 -> 4; matrix products, arithmetic and copies ran while one was open for 1% -> 0% of each run, Pallas kernels for 0% -> 0%
where the time goes in v1:
time: 316 us; the launch traced here: 315 us
  waiting for transfers between devices  137 us (43%)
  blocking collectives  78.6 us (25%)
  matrix products  38.7 us (12%)
  other arithmetic  26.3 us (8%)
  between operations  17.8 us (6%)
  local copies, waits for them, and re-layouts  9.85 us (3%)
  starting transfers between devices  6.59 us (2%)
    psum x5, blocking collectives, local(): lax.psum(v, axis)  53.1 us
    reduce_scatter x1, waiting for transfers between devices, sum_over_atoms(): part = lax.psum_scatter(payload, 'y', scatter_dimension=0, tiled=True)  43.4 us
    reduce_scatter x1, waiting for transfers between devices, local(): own = lax.psum_scatter(packed, KA_AXES, scatter_dimension=0, tiled=True)  35.5 us
    reduce_scatter x1, waiting for transfers between devices, sum_over_atoms(): part = lax.psum_scatter(part, 'x', scatter_dimension=0, tiled=True)  29.4 us
    all_to_all x1, waiting for transfers between devices, sum_over_atoms(): lax.all_to_all(jnp.stack([local_x] * lax.axis_size(which_axis)), which_ax...  28.8 us
    dot_general x1, matrix products, local(): jnp.dot(force_terms, k_vectors.T, precision=HIGHEST_PRECISION)  20.6 us
    slice x1, other arithmetic, local(): cosines = phases[:, :k_width].astype(jnp.float32)  17.6 us
    psum x1, blocking collectives, sum_over_atoms(): part = lax.psum(part, 'zh')  16.1 us
  transfers between devices with their start and end apart: 4, of which 4 were waited for; matrix products, arithmetic and copies ran while one was open for 0% of the time, Pallas kernels for 0%

profile of v1, /device:TPU:1, one launch (start us, length us, event | category | flops | bytes accessed | tf_op | source)
XLA Modules:
  0.0 315.0 jit_solution(17429110864755591134)
XLA Ops:
  7.2 0.0 reduce-scatter.4.cloned.1.call-start
  7.2 0.9 fusion.66
  8.1 0.7 convert_element_type.52
  9.5 1.6 fusion.69
  11.2 1.4 fusion.14
  12.6 1.7 convolution_add_fusion
  14.3 1.2 fusion.8
  15.5 0.6 fusion.65
  16.2 17.6 %cosine_convert_fusion = (bf16[2048,512]{1,0:T(8,128)(2,1)S(1)}, bf16[2048,512]{1,0:T(8,128)(2,1)S(1)}) fusion(f32[512]{0:T(512)S(1)} %bitcast.114, f32[2048]{0:T(1024)S(1)} %bitcast.106, f32[512]{0:T(512)S(1)} %bitcast.116, f32[2048]{0:T(1024)S(1)} %bitcast.108, f32[512]{0:T(512)S(1)} %bitcast.112, f32[2048]{0:T(1024)S(1)} %bitcast.104), kind=kLoop, calls=%fused_computation.8 | loop fusion | flops 8388608 | bytes 4225024 | tf_op jit(solution)/shard_map/slice | solution.py:168
  33.8 1.3 copy-done.4
  35.2 0.6 fusion.60
  35.8 3.0 concatenate.22
  38.9 1.0 reshape.321
  39.9 3.2 %fusion.15 = f32[1024,256]{1,0:T(8,128)S(1)} fusion(bf16[2048,256]{1,0:T(8,128)(2,1)S(1)} %copy-done.1, bf16[2048]{0:T(1024)(128)(2,1)S(1)} %fusion.41, bf16[2048,512]{1,0:T(8,128)(2,1)} %copy-done.4, bf16[2048,512]{1,0:T(8,128)(2,1)S(1)} %get-tuple-element.24), kind=kOutput, calls=%fused_computation.26 | convolution fusion | flops 1082654720 | bytes 6295552 | tf_op jit(solution)/shard_map/dot_general | solution.py:144
  43.2 1.1 pad_maximum_fusion.1
  44.3 0.0 reduce-scatter.4.cloned.1.call-update
  44.3 0.0 reduce-scatter.6.cloned.1.call-start
  44.4 43.4 %reduce-scatter.4.cloned.1.call-done = f32[160,256]{1,0:T(8,128)} async-done(((f32[1280,256]{1,0:T(8,128)}), f32[160,256]{1,0:T(8,128)}) %reduce-scatter.4.cloned.1.call-update) | async-done | bytes 163856 | tf_op jit(solution)/shard_map/reduce_scatter | solution.py:100
  87.8 0.0 reduce-scatter.6.cloned.1.call-update
  87.8 29.4 %reduce-scatter.6.cloned.1.call-done = f32[40,256]{1,0:T(8,128)} async-done(((f32[160,256]{1,0:T(8,128)}), f32[40,256]{1,0:T(8,128)}) %reduce-scatter.6.cloned.1.call-update) | async-done | bytes 40976 | tf_op jit(solution)/shard_map/reduce_scatter | solution.py:101
  117.2 16.1 %psum.42 = f32[40,256]{1,0:T(8,128)S(1)} all-reduce(f32[40,256]{1,0:T(8,128)} %reduce-scatter.6.cloned.1.call-done), channel_id=1, replica_groups=mesh['y'=8,'x'=4,'zh'=2,'zl'=4,'core'=2] {'zh'}, use_global_device_ids=true, to_apply=%region_2.3 | all-reduce | flops 10240 | bytes 81920 | tf_op jit(solution)/shard_map/psum | solution.py:102
  133.3 9.5 %all_gather.3 = f32[160,256]{1,0:T(8,128)S(1)} all-gather(f32[40,256]{1,0:T(8,128)S(1)} %psum.42), channel_id=1, replica_groups=mesh['y'=8,'x'=4,'zh'=2,'zl'=4,'core'=2] {'x'}, dimensions={0}, use_global_device_ids=true | all-gather | bytes 204800 | tf_op jit(solution)/shard_map/all_gather | solution.py:103
  142.8 1.2 stack.8
  143.9 6.5 %all-to-all-start = ((f32[8,160,256]{2,1,0:T(8,128)}), f32[8,160,256]{2,1,0:T(8,128)S(1)}, u32[]{:S(2)}, u32[]{:S(2)}) async-start(f32[8,160,256]{2,1,0:T(8,128)} %stack.8), calls=%async_computation.2 | async-start | bytes 2621440 | tf_op jit(solution)/shard_map/all_to_all | solution.py:105
  150.4 0.0 reduce-scatter.8.cloned.1.call-start
  151.1 0.1 pad.3.clone
  151.3 0.2 divide_multiply_fusion
  151.5 28.8 %all-to-all-done = f32[8,160,256]{2,1,0:T(8,128)S(1)} async-done(((f32[8,160,256]{2,1,0:T(8,128)}), f32[8,160,256]{2,1,0:T(8,128)S(1)}, u32[]{:S(2)}, u32[]{:S(2)}) %all-to-all-start) | async-done | bytes 1310752 | tf_op jit(solution)/shard_map/all_to_all | solution.py:105
  180.3 3.5 %fusion.59 = f32[2048,256]{0,1:T(8,128)S(1)} fusion(bf16[2048,512]{1,0:T(8,128)(2,1)} %copy-done.4, bf16[2048,512]{1,0:T(8,128)(2,1)} %copy-done.2, f32[1280,256]{1,0:T(8,128)S(1)} %bitcast.100, f32[512,256]{1,0:T(8,128)S(1)} %divide_multiply_fusion), kind=kOutput, calls=%fused_computation.99 | convolution fusion | flops 1082916864 | bytes 7864320 | tf_op jit(solution)/shard_map/dot_general | solution.py:163
  183.9 1.3 fusion.5
  185.2 20.6 %fusion.1 = f32[2048,3]{0,1:T(4,128)S(1)} fusion(f32[2048,1024]{1,0:T(8,128)S(1)} %fusion.5, s32[3,512]{1,0:T(4,128)S(1)} %copy-done.8, f32[512]{0:T(512)S(1)} %bitcast.115, f32[2048]{0:T(1024)S(1)} %bitcast.107, f32[512]{0:T(512)S(1)} %bitcast.117, f32[2048]{0:T(1024)S(1)} %bitcast.109, f32[512]{0:T(512)S(1)} %bitcast.113, f32[2048]{0:T(1024)S(1)} %bitcast.105), kind=kOutput, calls=%fused_computation.2 | convolution fusion | flops 51383296 | bytes 8450048 | tf_op jit(solution)/shard_map/dot_general | solution.py:171
  206.0 1.2 fusion.24
  207.1 1.6 maximum_maximum_fusion
  208.8 0.8 dynamic_slice.10
  209.5 35.5 %reduce-scatter.8.cloned.1.call-done = f32[256,264]{0,1:T(8,128)} async-done(((f32[2048,264]{0,1:T(8,128)}), f32[256,264]{0,1:T(8,128)}) %reduce-scatter.8.cloned.1.call-update) | async-done | bytes 270352 | tf_op jit(solution)/shard_map/reduce_scatter | solution.py:177
  245.0 1.0 multiply_reduce_fusion
  246.0 2.0 fusion.68
  248.0 0.3 fusion.70
  248.3 0.8 slice.127
  249.0 1.4 multiply_reduce_fusion.1
  250.4 1.9 multiply_reduce_fusion.2
  252.3 14.0 %psum.43 = f32[]{:T(128)} all-reduce(f32[]{:T(128)} %get-tuple-element.5), channel_id=1, replica_groups=mesh['y'=8,'x'=4,'zh'=2,'zl'=4,'core'=2] {'y'}, use_global_device_ids=true, to_apply=%region_7.8 | all-reduce | flops 1 | bytes 8 | tf_op jit(solution)/shard_map/psum | solution.py:196
  266.3 8.7 %psum.44 = f32[]{:T(128)} all-reduce(f32[]{:T(128)} %psum.43), channel_id=1, replica_groups=mesh['y'=8,'x'=4,'zh'=2,'zl'=4,'core'=2] {'x'}, use_global_device_ids=true, to_apply=%region_8.9 | all-reduce | flops 1 | bytes 8 | tf_op jit(solution)/shard_map/psum | solution.py:196
  275.0 8.3 %psum.45 = f32[]{:T(128)} all-reduce(f32[]{:T(128)} %psum.44), channel_id=1, replica_groups=mesh['y'=8,'x'=4,'zh'=2,'zl'=4,'core'=2] {'zh'}, use_global_device_ids=true, to_apply=%region_9.10 | all-reduce | flops 1 | bytes 8 | tf_op jit(solution)/shard_map/psum | solution.py:196
  283.3 0.1 copy.22
  283.5 11.5 %psum.46 = f32[]{:T(128)} all-reduce(f32[]{:T(128)} %psum.45), channel_id=1, replica_groups=mesh['y'=8,'x'=4,'zh'=2,'zl'=4,'core'=2] {'zl'}, use_global_device_ids=true, to_apply=%region_10.11 | all-reduce | flops 1 | bytes 8 | tf_op jit(solution)/shard_map/psum | solution.py:196
  294.9 0.5 slice.129
  295.4 10.6 %psum.47 = f32[]{:T(128)} all-reduce(f32[]{:T(128)} %psum.46), channel_id=1, replica_groups=mesh['y'=8,'x'=4,'zh'=2,'zl'=4,'core'=2] {'core'}, use_global_device_ids=true, to_apply=%region_11.12 | all-reduce | flops 1 | bytes 8 | tf_op jit(solution)/shard_map/psum | solution.py:196
  (57 shorter events, 0.3 us)
Async XLA Ops:
  7.2 238.8 %copy-start = (bf16[256,256]{1,0:T(8,128)(2,1)S(1)}, bf16[256,256]{1,0:T(8,128)(2,1)}, u32[]{:S(2)}) copy-start(bf16[256,256]{1,0:T(8,128)(2,1)} %param.23) | copy-start | bytes 393220
  7.2 7.1 %copy-start.19 = (f32[128]{0:T(128)S(1)}, f32[128]{0:T(128)}, u32[]{:S(2)}) copy-start(f32[128]{0:T(128)} %param.27) | copy-start | bytes 1540
  7.2 80.6 %reduce-scatter.4.cloned.1.call-start = ((), (), s32[]{:S(2)}) async-start(), calls=%async_computation.4 | async-start | bytes 1474560 | tf_op jit(solution)/shard_map/reduce_scatter | solution.py:100
  8.1 8.0 %copy-start.6 = (f32[1,2048]{1,0:T(1,128)}, f32[1,2048]{1,0:T(1,128)S(1)}, u32[]{:S(2)}) copy-start(f32[1,2048]{1,0:T(1,128)S(1)} %get-tuple-element.23) | copy-start | bytes 24580
  8.9 7.3 %copy-start.9 = (f32[1,512]{1,0:T(1,128)}, f32[1,512]{1,0:T(1,128)S(1)}, u32[]{:S(2)}) copy-start(f32[1,512]{1,0:T(1,128)S(1)} %get-tuple-element.34) | copy-start | bytes 6148
  8.9 7.3 %copy-start.11 = (f32[1,512]{1,0:T(1,128)}, f32[1,512]{1,0:T(1,128)S(1)}, u32[]{:S(2)}) copy-start(f32[1,512]{1,0:T(1,128)S(1)} %get-tuple-element.35) | copy-start | bytes 6148
  8.9 7.3 %copy-start.13 = (f32[1,512]{1,0:T(1,128)}, f32[1,512]{1,0:T(1,128)S(1)}, u32[]{:S(2)}) copy-start(f32[1,512]{1,0:T(1,128)S(1)} %get-tuple-element.36) | copy-start | bytes 6148
  33.8 1.3 copy-start.4
  33.8 9.3 %copy-start.2 = (bf16[2048,512]{1,0:T(8,128)(2,1)}, bf16[2048,512]{1,0:T(8,128)(2,1)S(1)}, u32[]{:S(2)}) copy-start(bf16[2048,512]{1,0:T(8,128)(2,1)S(1)} %get-tuple-element.24) | copy-start | bytes 6291460
  33.8 6.1 %copy-start.1 = (bf16[2048,256]{1,0:T(8,128)(2,1)S(1)}, bf16[2048,256]{1,0:T(8,128)(2,1)}, u32[]{:S(2)}) copy-start(bf16[2048,256]{1,0:T(8,128)(2,1)} %param.15) | copy-start | bytes 3145732
  44.3 106.8 %copy-start.15 = (f32[256]{0:T(256)S(1)}, f32[256]{0:T(256)}, u32[]{:S(2)}) copy-start(f32[256]{0:T(256)} %param.20) | copy-start | bytes 3076
  44.3 106.9 %copy-start.8 = (s32[3,512]{1,0:T(4,128)S(1)}, s32[3,512]{1,0:T(4,128)}, u32[]{:S(2)}) copy-start(s32[3,512]{1,0:T(4,128)} %param.17) | copy-start | bytes 18436
  44.3 72.9 %reduce-scatter.6.cloned.1.call-start = ((), (), s32[]{:S(2)}) async-start(), calls=%async_computation.5 | async-start | bytes 204800 | tf_op jit(solution)/shard_map/reduce_scatter | solution.py:101
  143.9 36.3 %all-to-all-start = ((f32[8,160,256]{2,1,0:T(8,128)}), f32[8,160,256]{2,1,0:T(8,128)S(1)}, u32[]{:S(2)}, u32[]{:S(2)}) async-start(f32[8,160,256]{2,1,0:T(8,128)} %stack.8), calls=%async_computation.2 | async-start | bytes 2621440 | tf_op jit(solution)/shard_map/all_to_all | solution.py:105
  150.4 94.6 %reduce-scatter.8.cloned.1.call-start = ((), (), s32[]{:S(2)}) async-start(), calls=%async_computation.6 | async-start | bytes 2433024 | tf_op jit(solution)/shard_map/reduce_scatter | solution.py:177
  180.3 3.5 %copy-start.16 = (f32[256]{0:T(256)S(1)}, f32[256]{0:T(256)}, u32[]{:S(2)}) copy-start(f32[256]{0:T(256)} %param.21) | copy-start | bytes 3076
  183.8 1.3 copy-start.7
  183.8 1.3 copy-start.10
  183.8 1.3 copy-start.12
  183.9 1.3 copy-start.14
  185.2 20.7 %copy-start.3 = (bf16[2048,512]{1,0:T(8,128)(2,1)S(1)}, bf16[2048,512]{1,0:T(8,128)(2,1)}, u32[]{:S(2)}) copy-start(bf16[2048,512]{1,0:T(8,128)(2,1)} %copy-done.2) | copy-start | bytes 6291460
  185.2 20.7 %copy-start.5 = (bf16[2048,512]{1,0:T(8,128)(2,1)S(1)}, bf16[2048,512]{1,0:T(8,128)(2,1)}, u32[]{:S(2)}) copy-start(bf16[2048,512]{1,0:T(8,128)(2,1)} %copy-done.4) | copy-start | bytes 6291460
  207.1 38.9 %copy-start.18 = (f32[256]{0:T(256)S(1)}, f32[256]{0:T(256)}, u32[]{:S(2)}) copy-start(f32[256]{0:T(256)} %param.22) | copy-start | bytes 3076
  207.1 40.9 %copy-start.17 = (f32[256]{0:T(256)S(1)}, f32[256]{0:T(256)}, u32[]{:S(2)}) copy-start(f32[256]{0:T(256)} %param.24) | copy-start | bytes 3076
Sparse Core Ops, SparseCore 0:
  44.5 43.2 reduce-scatter.3
  90.6 26.6 reduce-scatter.5
  208.9 36.0 reduce-scatter.7
